TPU v7x, 512 devices: a whole 4x4x16 slice. The times are simulated.
512 devices in a mesh: lon: 32 (over z, y_lo), lat: 16 (over y_hi, x, core).
Axes of the slice: x: 4, y: 4 (y_hi: 2, y_lo: 2; y = y_hi * 2 + y_lo), z: 16, core: 2. Of those that a mesh axis runs over, the one named last changes fastest.
Arguments:
- field: bfloat16 [2, 128, 128, 4096], P(None, 'lat', None, 'lon'), may hold values from -6 to 6
- weights: bfloat16 [2, 9, 128, 128], replicated, may hold values from -0.5 to 0.5
- coefs: bfloat16 [4, 128, 9, 4096], P(None, 'lat', None, 'lon'), may hold values from -2 to 2
- land_mask: int32 [2, 128, 4096], P(None, 'lat', 'lon'), may hold values 0 or 1
- fold_flag: int32 [128], replicated, may hold values from 0 to 1
Outputs:
- forward: bfloat16 [2, 128, 128, 4096], P(None, 'lat', None, 'lon')
- adjoint: bfloat16 [2, 128, 128, 4096], P(None, 'lat', None, 'lon')
Inputs may be any that keep to these rules, and one draw needn't show every extreme that they name: `land_mask`: 1 marks an ocean cell, 0 land. `fold_flag`: 1 marks a channel that holds a vector component, which changes sign across the north fold.
All inputs are finite; a program needn't handle non-finite values. No bound on the sum of `land_mask` on one device may be relied on, other than what follows from the above.
Results may differ from a plain program's by a relative error of at most 0.007.
Values may be sent and summed in bfloat16 or wider, within the bound.
No kernel may reach another device: no remote copies, remote signals or barrier semaphores. Data moves between devices by JAX's collectives and lax.ppermute only.
A program may use at most 64 MiB of HBM per device.

v0:
```python
import functools

import jax
import jax.numpy as jnp
from jax import lax
from jax.experimental import pallas as pl
from jax.experimental.pallas import tpu as pltpu
from jax.sharding import PartitionSpec as P

HALO = 4
PAD = 8


def exchange(block, fold_sign, taps, layers, channels):
    rows = block.shape[1]
    cols = block.shape[2]
    nlon = lax.axis_size("lon")
    nlat = lax.axis_size("lat")
    to_right = [(i, (i + 1) % nlon) for i in range(nlon)]
    to_left = [((i + 1) % nlon, i) for i in range(nlon)]
    from_left = lax.ppermute(block[:, :, cols - HALO :], "lon", to_right)
    from_right = lax.ppermute(block[:, :, :HALO], "lon", to_left)
    wide = jnp.concatenate([from_left, block, from_right], axis=2)

    to_up = [(j, j + 1) for j in range(nlat - 1)]
    to_down = [(j + 1, j) for j in range(nlat - 1)]
    below = lax.ppermute(wide[:, rows - HALO :], "lat", to_up)
    above = lax.ppermute(wide[:, :HALO], "lat", to_down)
    top = nlat - 1
    mirror_pairs = [(b * nlat + top, (nlon - 1 - b) * nlat + top) for b in range(nlon)]
    mirrored = lax.ppermute(wide[:, rows - HALO :], ("lon", "lat"), mirror_pairs)
    mirrored = mirrored[:, ::-1, ::-1]
    field_part = mirrored[..., :channels] * fold_sign
    coef_part = mirrored[..., channels : channels + layers * taps]
    coef_part = coef_part.reshape(coef_part.shape[:3] + (layers, taps))[..., ::-1].reshape(
        coef_part.shape
    )
    rest = mirrored[..., channels + layers * taps :]
    mirrored = jnp.concatenate([field_part, coef_part, rest], axis=3)
    is_top = lax.axis_index("lat") == top
    above = jnp.where(is_top, mirrored, above)
    return jnp.concatenate([below, wide, above], axis=1)


def stencil_kernel(x_ref, aux_ref, w_ref, o_ref, *, row_lo, row_hi, coef_lane, mask_lane, split, adjoint):
    levels = x_ref.shape[0]
    out_cols = x_ref.shape[2] - 2 * PAD
    chans = x_ref.shape[3]
    n = row_hi - row_lo
    o_ref[...] = jnp.zeros(o_ref.shape, o_ref.dtype)

    def body(idx, carry):
        lev = idx // n
        j = row_lo + idx % n
        acc = jnp.zeros((out_cols, chans), jnp.float32)
        for tap in range(w_ref.shape[1]):
            dj, di = tap // 3 - 1, tap % 3 - 1
            if adjoint:
                src = j - dj
                col = PAD - di
                xin = x_ref[lev, src, pl.ds(col, out_cols), :]
                xin = xin * aux_ref[lev, src, pl.ds(col, out_cols), pl.ds(mask_lane, 1)]
                cf = aux_ref[lev, src, pl.ds(col, out_cols), pl.ds(coef_lane + tap, 1)]
                sel = (src >= split).astype(jnp.int32)
            else:
                src = j + dj
                col = PAD + di
                xin = x_ref[lev, src, pl.ds(col, out_cols), :]
                cf = aux_ref[lev, j, pl.ds(PAD, out_cols), pl.ds(coef_lane + tap, 1)]
                sel = (j >= split).astype(jnp.int32)
            prod = jnp.dot(
                xin.astype(jnp.bfloat16), w_ref[sel, tap], preferred_element_type=jnp.float32
            )
            acc = acc + cf * prod
        if not adjoint:
            acc = acc * aux_ref[lev, j, pl.ds(PAD, out_cols), pl.ds(mask_lane, 1)]
        o_ref[lev, j, pl.ds(PAD, out_cols), :] = acc.astype(jnp.bfloat16).astype(jnp.float32)
        return carry

    lax.fori_loop(0, levels * n, body, 0)


def stencil(x, aux, w, row_lo, row_hi, coef_lane, mask_lane, split, adjoint):
    kernel = functools.partial(
        stencil_kernel,
        row_lo=row_lo,
        row_hi=row_hi,
        coef_lane=coef_lane,
        mask_lane=mask_lane,
        split=split,
        adjoint=adjoint,
    )
    levels, _, width, chans = x.shape
    rows_done = row_hi - row_lo
    flops = 2 * levels * rows_done * (width - 2 * PAD) * chans * chans * w.shape[1]
    return pl.pallas_call(
        kernel,
        out_shape=jax.ShapeDtypeStruct(x.shape, jnp.float32),
        in_specs=[pl.BlockSpec(memory_space=pltpu.VMEM)] * 3,
        out_specs=pl.BlockSpec(memory_space=pltpu.VMEM),
        cost_estimate=pl.CostEstimate(
            flops=flops, bytes_accessed=2 * x.size * 4 + aux.size * 4, transcendentals=0
        ),
    )(x, aux, w)


def local(field, weights, coefs, land_mask, fold_flag):
    layers, taps = weights.shape[0], weights.shape[1]
    levels, rows, channels, cols = field.shape
    fold_sign = jnp.where(fold_flag == 1, -1.0, 1.0).astype(jnp.bfloat16)
    coef_stack = (
        coefs.reshape(layers, levels, rows, taps, cols)
        .transpose(1, 2, 4, 0, 3)
        .reshape(levels, rows, cols, layers * taps)
    )
    mask_stack = land_mask.astype(jnp.bfloat16)[..., None]
    block = jnp.concatenate([field.transpose(0, 1, 3, 2), coef_stack, mask_stack], axis=3)
    ext = exchange(block, fold_sign, taps, layers, channels)
    ext = jnp.pad(ext, ((0, 0), (0, 0), (PAD, PAD), (0, 0))).astype(jnp.float32)
    x = ext[..., :channels]
    aux = ext[..., channels:]
    mask_lane = layers * taps

    is_top = lax.axis_index("lat") == lax.axis_size("lat") - 1
    flipped = weights[:, ::-1] * fold_sign[None, None, :, None] * fold_sign[None, None, None, :]
    weights_high = jnp.where(is_top, flipped, weights)
    both = jnp.stack([weights, weights_high], axis=1)
    forward_w = both.transpose(0, 1, 2, 4, 3)

    split = HALO + rows
    total_rows = ext.shape[1]
    current = x
    for layer in range(layers):
        current = stencil(
            current,
            aux,
            forward_w[layer],
            layer + 1,
            total_rows - layer - 1,
            layer * taps,
            mask_lane,
            split,
            False,
        )
    forward_rows = current[:, HALO : HALO + rows, PAD + HALO : PAD + HALO + cols]
    forward = forward_rows.transpose(0, 1, 3, 2).astype(jnp.bfloat16)
    adjoint_now = current
    depth = layers
    for layer in reversed(range(layers)):
        depth += 1
        adjoint_now = stencil(
            adjoint_now,
            aux,
            both[layer],
            depth,
            total_rows - depth,
            layer * taps,
            mask_lane,
            split,
            True,
        )
    adjoint_rows = adjoint_now[:, HALO : HALO + rows, PAD + HALO : PAD + HALO + cols]
    return (forward, adjoint_rows.transpose(0, 1, 3, 2).astype(jnp.bfloat16))


def solution(mesh):
    return jax.shard_map(
        local,
        mesh=mesh,
        in_specs=(
            P(None, "lat", None, "lon"),
            P(),
            P(None, "lat", None, "lon"),
            P(None, "lat", "lon"),
            P(),
        ),
        out_specs=(P(None, "lat", None, "lon"), P(None, "lat", None, "lon")),
        check_vma=False,
    )
```

profile of v0, /device:TPU:31, one launch (start us, length us, event | category | flops | bytes accessed | tf_op | source)
XLA Modules:
  0.0 123.4 jit_solution(7015313282819082092)
XLA Ops:
  0.6 0.0 copy-start.1
  0.6 0.0 copy-start
  0.7 0.8 convert_bitcast_fusion
  1.4 0.3 copy.25
  1.7 0.9 copy.23
  2.6 0.3 copy.24
  2.9 1.3 %copy.22 = bf16[2,8,128,128]{2,3,1,0:T(8,128)(2,1)S(1)} copy(bf16[2,8,128,128]{3,2,1,0:T(8,128)(2,1)} %param.5) | data formatting | bytes 1048576 | tf_op args[0]
  4.3 0.1 pad_maximum_fusion.4
  4.4 2.4 %collective-permute-start.1 = (bf16[2,8,4,147]{3,2,1,0:T(4,128)(2,1)S(1)}, bf16[2,8,4,147]{3,2,1,0:T(4,128)(2,1)S(1)}, u32[]{:S(2)}, u32[]{:S(2)}) collective-permute-start(bf16[2,8,4,147]{3,2,1,0:T(4,128)(2,1)S(1)} %get-tuple-element.9), channel_id=1, source_target_pairs={{16,0},{32,16},{48,32},{64,48},{80,64},{96,80},{112,96},{128,112},... | collective-permute-start | bytes 56456 | tf_op jit(solution)/shard_map/ppermute | solution.py:22
  6.7 3.8 %collective-permute-start = (bf16[2,8,4,147]{3,2,1,0:T(4,128)(2,1)S(1)}, bf16[2,8,4,147]{3,2,1,0:T(4,128)(2,1)S(1)}, u32[]{:S(2)}, u32[]{:S(2)}) collective-permute-start(bf16[2,8,4,147]{3,2,1,0:T(4,128)(2,1)S(1)} %get-tuple-element.8), channel_id=1, source_target_pairs={{0,16},{16,32},{32,48},{48,64},{64,80},{80,96},{96,112},{112,128},... | collective-permute-start | bytes 56456 | tf_op jit(solution)/shard_map/ppermute | solution.py:21
  10.6 0.0 copy-done.1
  10.6 0.0 copy-done
  10.6 0.3 select_bitcast_fusion
  10.9 0.1 fusion.11
  11.0 0.0 collective-permute-done.1
  11.0 8.8 %collective-permute-done = bf16[2,8,4,147]{3,2,1,0:T(4,128)(2,1)S(1)} collective-permute-done((bf16[2,8,4,147]{3,2,1,0:T(4,128)(2,1)S(1)}, bf16[2,8,4,147]{3,2,1,0:T(4,128)(2,1)S(1)}, u32[]{:S(2)}, u32[]{:S(2)}) %collective-permute-start) | collective-permute-done | bytes 18848 | tf_op jit(solution)/shard_map/ppermute | solution.py:21
  19.9 0.6 pad_maximum_fusion.1
  20.5 1.1 fusion.19
  21.6 4.7 %collective-permute-start.3 = (bf16[2,4,136,147]{3,2,1,0:T(8,128)(2,1)}, bf16[2,4,136,147]{3,2,1,0:T(8,128)(2,1)}, u32[]{:S(2)}, u32[]{:S(2)}) collective-permute-start(bf16[2,4,136,147]{3,2,1,0:T(8,128)(2,1)} %get-tuple-element.14), channel_id=1, source_target_pairs={{15,511},{31,495},{47,479},{63,463},{79,447},{95,431},{111,415},{1... | collective-permute-start | bytes 959624 | tf_op jit(solution)/shard_map/ppermute | solution.py:31
  26.3 0.9 slice_bitcast_fusion
  27.2 2.1 %copy.28.w_ref = bf16[2,9,128,128]{3,2,1,0:T(8,128)(2,1)} copy(bf16[2,9,128,128]{2,3,1,0:T(8,128)(2,1)} %get-tuple-element.13) | data formatting | bytes 1179648 | tf_op jit(solution)/shard_map/squeeze | solution.py:137
  29.4 1.2 copy.29.w_ref
  30.5 1.3 %collective-permute-start.4 = (bf16[2,4,136,147]{3,2,1,0:T(8,128)(2,1)}, bf16[2,4,136,147]{3,2,1,0:T(8,128)(2,1)S(1)}, u32[]{:S(2)}, u32[]{:S(2)}) collective-permute-start(bf16[2,4,136,147]{3,2,1,0:T(8,128)(2,1)} %get-tuple-element.15), channel_id=1, source_target_pairs={{1,0},{2,1},{3,2},{4,3},{5,4},{6,5},{7,6},{8,7},{9,8},{10,9},{11,1... | collective-permute-start | bytes 959624 | tf_op jit(solution)/shard_map/ppermute | solution.py:28
  31.8 1.2 fusion.15
  33.1 1.3 %collective-permute-start.2 = (bf16[2,4,136,147]{3,2,1,0:T(8,128)(2,1)}, bf16[2,4,136,147]{3,2,1,0:T(8,128)(2,1)}, u32[]{:S(2)}, u32[]{:S(2)}) collective-permute-start(bf16[2,4,136,147]{3,2,1,0:T(8,128)(2,1)} %get-tuple-element.14), channel_id=1, source_target_pairs={{0,1},{1,2},{2,3},{3,4},{4,5},{5,6},{6,7},{7,8},{8,9},{9,10},{10,1... | collective-permute-start | bytes 959624 | tf_op jit(solution)/shard_map/ppermute | solution.py:27
  34.4 17.5 %collective-permute-done.3 = bf16[2,4,136,147]{3,2,1,0:T(8,128)(2,1)} collective-permute-done((bf16[2,4,136,147]{3,2,1,0:T(8,128)(2,1)}, bf16[2,4,136,147]{3,2,1,0:T(8,128)(2,1)}, u32[]{:S(2)}, u32[]{:S(2)}) %collective-permute-start.3) | collective-permute-done | bytes 319904 | tf_op jit(solution)/shard_map/ppermute | solution.py:31
  51.9 1.0 slice.76
  52.9 1.0 slice.61
  53.9 1.1 slice.78
  55.0 1.0 slice.65
  56.0 1.0 slice.77
  57.0 1.0 slice.63
  58.0 0.2 copy.26
  58.3 0.3 copy.27
  58.6 0.0 collective-permute-done.4
  58.6 0.2 maximum_select_fusion
  58.8 0.0 collective-permute-done.2
  58.8 2.1 %fusion.1 = f32[2,16,152,147]{3,2,1,0:T(8,128)S(1)} fusion(bf16[2,4,136,147]{3,2,1,0:T(8,128)(2,1)S(1)} %maximum_select_fusion, bf16[2,4,136,147]{3,2,1,0:T(8,128)(2,1)} %collective-permute-done.2, bf16[2,8,4,147]{3,2,1,0:T(4,128)(2,1)S(1)} %collective-permute-done.1, bf16[2,8,4,147]{3,2,1,0:T(4,128)(2,1)S(1)} %collective-permute-done, ...), kind=kLoop, calls=%fused_computation.4 | loop fusion | flops 17160192 | bytes 4139520 | tf_op jit(solution)/shard_map/convert_element_type | solution.py:119
  61.0 1.7 %slice.80.x_ref = f32[2,16,152,128]{3,2,1,0:T(8,128)} slice(f32[2,16,152,147]{3,2,1,0:T(8,128)S(1)} %fusion.1), slice={[0:2], [0:16], [0:152], [0:128]} | slice | bytes 4980736 | tf_op jit(solution)/shard_map/slice | solution.py:120
  62.6 1.6 %slice.81.aux_ref = f32[2,16,152,19]{3,2,1,0:T(8,128)} slice(f32[2,16,152,147]{3,2,1,0:T(8,128)S(1)} %fusion.1), slice={[0:2], [0:16], [0:152], [128:147]} | slice | bytes 739328 | tf_op jit(solution)/shard_map/slice | solution.py:121
  64.2 14.1 %shard_map.68.x_ref = f32[2,16,152,128]{3,2,1,0:T(8,128)} custom-call(f32[2,16,152,128]{3,2,1,0:T(8,128)} %slice.80.x_ref, f32[2,16,152,19]{3,2,1,0:T(8,128)} %slice.81.aux_ref, bf16[2,9,128,128]{3,2,1,0:T(8,128)(2,1)} %copy.28.w_ref), custom_call_target="tpu_custom_call" | custom-call | flops 1123024896 | bytes 5350400 | tf_op jit(solution)/shard_map/pallas_call | solution.py:96
  78.4 12.8 %shard_map.69.x_ref = f32[2,16,152,128]{3,2,1,0:T(8,128)} custom-call(f32[2,16,152,128]{3,2,1,0:T(8,128)} %shard_map.68.x_ref, f32[2,16,152,19]{3,2,1,0:T(8,128)} %slice.81.aux_ref, bf16[2,9,128,128]{3,2,1,0:T(8,128)(2,1)} %copy.29.w_ref), custom_call_target="tpu_custom_call" | custom-call | flops 962592768 | bytes 5350400 | tf_op jit(solution)/shard_map/pallas_call | solution.py:96
  91.1 1.4 %fusion.16 = bf16[2,8,128,128]{2,3,1,0:T(8,128)(2,1)S(1)} fusion(f32[2,16,152,128]{3,2,1,0:T(8,128)} %shard_map.69.x_ref), kind=kLoop, calls=%fused_computation.32 | loop fusion | bytes 1048576 | tf_op jit(solution)/shard_map/convert_element_type | solution.py:146
  92.5 1.0 copy.30
  93.5 14.8 %shard_map.70.x_ref = f32[2,16,152,128]{3,2,1,0:T(8,128)} custom-call(f32[2,16,152,128]{3,2,1,0:T(8,128)} %shard_map.69.x_ref, f32[2,16,152,19]{3,2,1,0:T(8,128)} %slice.81.aux_ref, bf16[2,9,128,128]{3,2,1,0:T(8,128)(2,1)} %get-tuple-element.11.w_ref), custom_call_target="tpu_custom_call" | custom-call | flops 802160640 | bytes 5350400 | tf_op jit(solution)/shard_map/pallas_call | solution.py:96
  108.4 12.6 %shard_map.71 = f32[2,16,152,128]{3,2,1,0:T(8,128)} custom-call(f32[2,16,152,128]{3,2,1,0:T(8,128)} %shard_map.70.x_ref, f32[2,16,152,19]{3,2,1,0:T(8,128)} %slice.81.aux_ref, bf16[2,9,128,128]{3,2,1,0:T(8,128)(2,1)} %get-tuple-element.10.w_ref), custom_call_target="tpu_custom_call" | custom-call | flops 641728512 | bytes 5350400 | tf_op jit(solution)/shard_map/pallas_call | solution.py:96
  121.0 1.4 %fusion.17 = bf16[2,8,128,128]{2,3,1,0:T(8,128)(2,1)S(1)} fusion(f32[2,16,152,128]{3,2,1,0:T(8,128)} %shard_map.71), kind=kLoop, calls=%fused_computation.33 | loop fusion | bytes 1048576 | tf_op jit(solution)/shard_map/convert_element_type | solution.py:163
  122.4 1.0 copy.31
  (3 shorter events, 0.1 us)
Async XLA Ops:
  0.6 9.9 %copy-start.1 = (s32[128]{0:T(128)S(1)}, s32[128]{0:T(128)}, u32[]{:S(2)}) copy-start(s32[128]{0:T(128)} %param.9) | copy-start | bytes 1540
  0.6 10.0 %copy-start = (bf16[2,9,128,128]{3,2,1,0:T(8,128)(2,1)S(1)}, bf16[2,9,128,128]{3,2,1,0:T(8,128)(2,1)}, u32[]{:S(2)}) copy-start(bf16[2,9,128,128]{3,2,1,0:T(8,128)(2,1)} %param.6) | copy-start | bytes 1769476
  4.4 6.7 %collective-permute-start.1 = (bf16[2,8,4,147]{3,2,1,0:T(4,128)(2,1)S(1)}, bf16[2,8,4,147]{3,2,1,0:T(4,128)(2,1)S(1)}, u32[]{:S(2)}, u32[]{:S(2)}) collective-permute-start(bf16[2,8,4,147]{3,2,1,0:T(4,128)(2,1)S(1)} %get-tuple-element.9), channel_id=1, source_target_pairs={{16,0},{32,16},{48,32},{64,48},{80,64},{96,80},{112,96},{128,112},... | collective-permute-start | bytes 56456 | tf_op jit(solution)/shard_map/ppermute | solution.py:22
  6.7 13.1 %collective-permute-start = (bf16[2,8,4,147]{3,2,1,0:T(4,128)(2,1)S(1)}, bf16[2,8,4,147]{3,2,1,0:T(4,128)(2,1)S(1)}, u32[]{:S(2)}, u32[]{:S(2)}) collective-permute-start(bf16[2,8,4,147]{3,2,1,0:T(4,128)(2,1)S(1)} %get-tuple-element.8), channel_id=1, source_target_pairs={{0,16},{16,32},{32,48},{48,64},{64,80},{80,96},{96,112},{112,128},... | collective-permute-start | bytes 56456 | tf_op jit(solution)/shard_map/ppermute | solution.py:21
  21.6 30.3 %collective-permute-start.3 = (bf16[2,4,136,147]{3,2,1,0:T(8,128)(2,1)}, bf16[2,4,136,147]{3,2,1,0:T(8,128)(2,1)}, u32[]{:S(2)}, u32[]{:S(2)}) collective-permute-start(bf16[2,4,136,147]{3,2,1,0:T(8,128)(2,1)} %get-tuple-element.14), channel_id=1, source_target_pairs={{15,511},{31,495},{47,479},{63,463},{79,447},{95,431},{111,415},{1... | collective-permute-start | bytes 959624 | tf_op jit(solution)/shard_map/ppermute | solution.py:31
  30.5 28.0 %collective-permute-start.4 = (bf16[2,4,136,147]{3,2,1,0:T(8,128)(2,1)}, bf16[2,4,136,147]{3,2,1,0:T(8,128)(2,1)S(1)}, u32[]{:S(2)}, u32[]{:S(2)}) collective-permute-start(bf16[2,4,136,147]{3,2,1,0:T(8,128)(2,1)} %get-tuple-element.15), channel_id=1, source_target_pairs={{1,0},{2,1},{3,2},{4,3},{5,4},{6,5},{7,6},{8,7},{9,8},{10,9},{11,1... | collective-permute-start | bytes 959624 | tf_op jit(solution)/shard_map/ppermute | solution.py:28
  33.1 25.8 %collective-permute-start.2 = (bf16[2,4,136,147]{3,2,1,0:T(8,128)(2,1)}, bf16[2,4,136,147]{3,2,1,0:T(8,128)(2,1)}, u32[]{:S(2)}, u32[]{:S(2)}) collective-permute-start(bf16[2,4,136,147]{3,2,1,0:T(8,128)(2,1)} %get-tuple-element.14), channel_id=1, source_target_pairs={{0,1},{1,2},{2,3},{3,4},{4,5},{5,6},{6,7},{7,8},{8,9},{9,10},{10,1... | collective-permute-start | bytes 959624 | tf_op jit(solution)/shard_map/ppermute | solution.py:27
where the time goes:
time: 124 us; the launch traced here: 123 us
  Pallas kernels  54.4 us (44%)
  waiting for transfers between devices  26.4 us (21%)
  local copies, waits for them, and re-layouts  22.8 us (18%)
  starting transfers between devices  13.5 us (11%)
  other arithmetic  5.54 us (4%)
    pallas_call x4, Pallas kernels, stencil(): pl.pallas_call(kernel, out_shape=jax.ShapeDtypeStruct(x.shape, jnp.float3...  54.4 us
    ppermute x1, waiting for transfers between devices, exchange(): mirrored = lax.ppermute(wide[:, rows - HALO:], ('lon', 'lat'), mirror_pairs)  17.5 us
    ppermute x1, waiting for transfers between devices, exchange(): from_left = lax.ppermute(block[:, :, cols - HALO:], 'lon', to_right)  8.85 us
    ppermute x1, starting transfers between devices, exchange(): mirrored = lax.ppermute(wide[:, rows - HALO:], ('lon', 'lat'), mirror_pairs)  4.69 us
    squeeze x3, local copies, waits for them, and re-layouts, local(): forward_w[layer]  4.19 us
    ppermute x1, starting transfers between devices, exchange(): from_left = lax.ppermute(block[:, :, cols - HALO:], 'lon', to_right)  3.81 us
    unnamed x7, local copies, waits for them, and re-layouts  3.34 us
  transfers between devices with their start and end apart: 5, of which 2 were waited for; matrix products, arithmetic and copies ran while one was open for 10% of the time, Pallas kernels for 0%

commit v1 on v0

--- a/solution.py
+++ b/solution.py
@@ -42,42 +42,54 @@
     return jnp.concatenate([below, wide, above], axis=1)
 
 
-def stencil_kernel(x_ref, aux_ref, w_ref, o_ref, *, row_lo, row_hi, coef_lane, mask_lane, split, adjoint):
+def stencil_kernel(x_ref, aux_ref, w_ref, o_ref, acc_ref, *, row_lo, row_hi, coef_lane, mask_lane, split, adjoint):
     levels = x_ref.shape[0]
     out_cols = x_ref.shape[2] - 2 * PAD
     chans = x_ref.shape[3]
-    n = row_hi - row_lo
     o_ref[...] = jnp.zeros(o_ref.shape, o_ref.dtype)
 
-    def body(idx, carry):
-        lev = idx // n
-        j = row_lo + idx % n
-        acc = jnp.zeros((out_cols, chans), jnp.float32)
+    def level_body(lev, carry):
+        acc_ref[...] = jnp.zeros(acc_ref.shape, acc_ref.dtype)
         for tap in range(w_ref.shape[1]):
             dj, di = tap // 3 - 1, tap % 3 - 1
+            step = -dj if adjoint else dj
+            col = PAD - di if adjoint else PAD + di
             if adjoint:
-                src = j - dj
-                col = PAD - di
-                xin = x_ref[lev, src, pl.ds(col, out_cols), :]
-                xin = xin * aux_ref[lev, src, pl.ds(col, out_cols), pl.ds(mask_lane, 1)]
-                cf = aux_ref[lev, src, pl.ds(col, out_cols), pl.ds(coef_lane + tap, 1)]
-                sel = (src >= split).astype(jnp.int32)
+                groups = ((row_lo, min(row_hi, split + dj), 0), (max(row_lo, split + dj), row_hi, 1))
             else:
-                src = j + dj
-                col = PAD + di
-                xin = x_ref[lev, src, pl.ds(col, out_cols), :]
-                cf = aux_ref[lev, j, pl.ds(PAD, out_cols), pl.ds(coef_lane + tap, 1)]
-                sel = (j >= split).astype(jnp.int32)
-            prod = jnp.dot(
-                xin.astype(jnp.bfloat16), w_ref[sel, tap], preferred_element_type=jnp.float32
-            )
-            acc = acc + cf * prod
+                groups = ((row_lo, min(row_hi, split), 0), (max(row_lo, split), row_hi, 1))
+            for lo, hi, sel in groups:
+                if hi <= lo:
+                    continue
+                count = hi - lo
+                src = slice(lo + step, hi + step)
+                xin = x_ref[lev, src, pl.ds(col, out_cols), :].reshape(count * out_cols, chans)
+                if adjoint:
+                    mask_col = aux_ref[lev, src, pl.ds(col, out_cols), pl.ds(mask_lane, 1)]
+                    xin = xin * mask_col.reshape(count * out_cols, 1)
+                    cf = aux_ref[lev, src, pl.ds(col, out_cols), pl.ds(coef_lane + tap, 1)]
+                    prod = jnp.dot(
+                        xin.astype(jnp.bfloat16), w_ref[sel, tap], preferred_element_type=jnp.float32
+                    )
+                else:
+                    cf = aux_ref[lev, lo:hi, pl.ds(PAD, out_cols), pl.ds(coef_lane + tap, 1)]
+                    prod = lax.dot_general(
+                        xin.astype(jnp.bfloat16),
+                        w_ref[sel, tap],
+                        (((1,), (1,)), ((), ())),
+                        preferred_element_type=jnp.float32,
+                    )
+                term = cf.reshape(count * out_cols, 1) * prod
+                acc_ref[lo:hi] += term.reshape(count, out_cols, chans)
+        result = acc_ref[row_lo:row_hi]
         if not adjoint:
-            acc = acc * aux_ref[lev, j, pl.ds(PAD, out_cols), pl.ds(mask_lane, 1)]
-        o_ref[lev, j, pl.ds(PAD, out_cols), :] = acc.astype(jnp.bfloat16).astype(jnp.float32)
+            result = result * aux_ref[lev, row_lo:row_hi, pl.ds(PAD, out_cols), pl.ds(mask_lane, 1)]
+        o_ref[lev, row_lo:row_hi, pl.ds(PAD, out_cols), :] = result.astype(jnp.bfloat16).astype(
+            jnp.float32
+        )
         return carry
 
-    lax.fori_loop(0, levels * n, body, 0)
+    lax.fori_loop(0, levels, level_body, 0)
 
 
 def stencil(x, aux, w, row_lo, row_hi, coef_lane, mask_lane, split, adjoint):
@@ -90,7 +102,7 @@
         split=split,
         adjoint=adjoint,
     )
-    levels, _, width, chans = x.shape
+    levels, total_rows, width, chans = x.shape
     rows_done = row_hi - row_lo
     flops = 2 * levels * rows_done * (width - 2 * PAD) * chans * chans * w.shape[1]
     return pl.pallas_call(
@@ -98,6 +110,7 @@
         out_shape=jax.ShapeDtypeStruct(x.shape, jnp.float32),
         in_specs=[pl.BlockSpec(memory_space=pltpu.VMEM)] * 3,
         out_specs=pl.BlockSpec(memory_space=pltpu.VMEM),
+        scratch_shapes=[pltpu.VMEM((total_rows, width - 2 * PAD, chans), jnp.float32)],
         cost_estimate=pl.CostEstimate(
             flops=flops, bytes_accessed=2 * x.size * 4 + aux.size * 4, transcendentals=0
         ),
@@ -125,7 +138,6 @@
     flipped = weights[:, ::-1] * fold_sign[None, None, :, None] * fold_sign[None, None, None, :]
     weights_high = jnp.where(is_top, flipped, weights)
     both = jnp.stack([weights, weights_high], axis=1)
-    forward_w = both.transpose(0, 1, 2, 4, 3)
 
     split = HALO + rows
     total_rows = ext.shape[1]
@@ -134,7 +146,7 @@
         current = stencil(
             current,
             aux,
-            forward_w[layer],
+            both[layer],
             layer + 1,
             total_rows - layer - 1,
             layer * taps,

time: 124 us -> 106 us (0.85)
  Pallas kernels: 54.4 us -> 39.4 us
  local copies, waits for them, and re-layouts: 22.8 us -> 15.5 us
  waiting for transfers between devices: 26.4 us -> 29.5 us
    pallas_call x4, Pallas kernels: 54.4 us -> 39.4 us  [stencil(): pl.pallas_call(kernel, out_shape=jax.ShapeDtypeStruct(x.shape, jnp.float3...]
    squeeze x3 -> x0, local copies, waits for them, and re-layouts: 4.19 us -> none  [local(): forward_w[layer]]
    ppermute x1, waiting for transfers between devices: 17.5 us -> 20.2 us  [exchange(): mirrored = lax.ppermute(wide[:, rows - HALO:], ('lon', 'lat'), mirror_pairs)]
    unnamed x7 -> x11, local copies, waits for them, and re-layouts: 3.34 us -> 3.35 us
  transfers between devices with their start and end apart: 5 -> 5, of which waited for: 2 -> 2; matrix products, arithmetic and copies ran while one was open for 10% -> 5% of each run, Pallas kernels for 0% -> 0%
where the time goes in v1:
time: 106 us; the launch traced here: 105 us
  Pallas kernels  39.4 us (37%)
  waiting for transfers between devices  29.5 us (28%)
  local copies, waits for them, and re-layouts  15.5 us (15%)
  starting transfers between devices  14.4 us (14%)
  other arithmetic  5.28 us (5%)
    pallas_call x4, Pallas kernels, stencil(): pl.pallas_call(kernel, out_shape=jax.ShapeDtypeStruct(x.shape, jnp.float3...  39.4 us
    ppermute x1, waiting for transfers between devices, exchange(): mirrored = lax.ppermute(wide[:, rows - HALO:], ('lon', 'lat'), mirror_pairs)  20.2 us
    ppermute x1, waiting for transfers between devices, exchange(): from_left = lax.ppermute(block[:, :, cols - HALO:], 'lon', to_right)  9.27 us
    ppermute x1, starting transfers between devices, exchange(): mirrored = lax.ppermute(wide[:, rows - HALO:], ('lon', 'lat'), mirror_pairs)  4.69 us
    ppermute x1, starting transfers between devices, exchange(): from_left = lax.ppermute(block[:, :, cols - HALO:], 'lon', to_right)  3.81 us
    unnamed x11, local copies, waits for them, and re-layouts  3.35 us
    ppermute x1, starting transfers between devices, exchange(): from_right = lax.ppermute(block[:, :, :HALO], 'lon', to_left)  2.37 us
    convert_element_type x1, other arithmetic, local(): ext = jnp.pad(ext, ((0, 0), (0, 0), (PAD, PAD), (0, 0))).astype(jnp.float32)  2.12 us
  transfers between devices with their start and end apart: 5, of which 2 were waited for; matrix products, arithmetic and copies ran while one was open for 5% of the time, Pallas kernels for 0%

profile of v1, /device:TPU:31, one launch (start us, length us, event | category | flops | bytes accessed | tf_op | source)
XLA Modules:
  0.0 105.1 jit_solution(16731714688567318033)
XLA Ops:
  0.6 0.0 copy-start.3
  0.6 0.7 convert_bitcast_fusion
  1.3 0.3 copy.21
  1.7 0.9 copy.19
  2.6 0.3 copy.20
  2.9 1.3 %copy.18 = bf16[2,8,128,128]{2,3,1,0:T(8,128)(2,1)S(1)} copy(bf16[2,8,128,128]{3,2,1,0:T(8,128)(2,1)} %param.5) | data formatting | bytes 1048576 | tf_op args[0]
  4.2 0.1 pad_maximum_fusion.4
  4.3 2.4 %collective-permute-start.1 = (bf16[2,8,4,147]{3,2,1,0:T(4,128)(2,1)S(1)}, bf16[2,8,4,147]{3,2,1,0:T(4,128)(2,1)S(1)}, u32[]{:S(2)}, u32[]{:S(2)}) collective-permute-start(bf16[2,8,4,147]{3,2,1,0:T(4,128)(2,1)S(1)} %get-tuple-element.9), channel_id=1, source_target_pairs={{16,0},{32,16},{48,32},{64,48},{80,64},{96,80},{112,96},{128,112},... | collective-permute-start | bytes 56456 | tf_op jit(solution)/shard_map/ppermute | solution.py:22
  6.7 3.8 %collective-permute-start = (bf16[2,8,4,147]{3,2,1,0:T(4,128)(2,1)S(1)}, bf16[2,8,4,147]{3,2,1,0:T(4,128)(2,1)S(1)}, u32[]{:S(2)}, u32[]{:S(2)}) collective-permute-start(bf16[2,8,4,147]{3,2,1,0:T(4,128)(2,1)S(1)} %get-tuple-element.8), channel_id=1, source_target_pairs={{0,16},{16,32},{32,48},{48,64},{64,80},{80,96},{96,112},{112,128},... | collective-permute-start | bytes 56456 | tf_op jit(solution)/shard_map/ppermute | solution.py:21
  10.5 0.0 copy-done.3
  10.5 0.0 copy-start
  10.5 0.0 collective-permute-done.1
  10.6 9.3 %collective-permute-done = bf16[2,8,4,147]{3,2,1,0:T(4,128)(2,1)S(1)} collective-permute-done((bf16[2,8,4,147]{3,2,1,0:T(4,128)(2,1)S(1)}, bf16[2,8,4,147]{3,2,1,0:T(4,128)(2,1)S(1)}, u32[]{:S(2)}, u32[]{:S(2)}) %collective-permute-start) | collective-permute-done | bytes 18848 | tf_op jit(solution)/shard_map/ppermute | solution.py:21
  19.8 0.0 copy-start.1
  19.8 0.6 pad_maximum_fusion
  20.5 0.9 fusion.17
  21.4 0.0 copy-done.1
  21.4 4.7 %collective-permute-start.3 = (bf16[2,4,136,147]{3,2,1,0:T(8,128)(2,1)S(1)}, bf16[2,4,136,147]{3,2,1,0:T(8,128)(2,1)S(1)}, u32[]{:S(2)}, u32[]{:S(2)}) collective-permute-start(bf16[2,4,136,147]{3,2,1,0:T(8,128)(2,1)S(1)} %get-tuple-element.12), channel_id=1, source_target_pairs={{15,511},{31,495},{47,479},{63,463},{79,447},{95,431},{111,415},{1... | collective-permute-start | bytes 959624 | tf_op jit(solution)/shard_map/ppermute | solution.py:31
  26.1 0.0 copy-done
  26.1 0.3 select_bitcast_fusion
  26.4 2.1 %collective-permute-start.4 = (bf16[2,4,136,147]{3,2,1,0:T(8,128)(2,1)}, bf16[2,4,136,147]{3,2,1,0:T(8,128)(2,1)}, u32[]{:S(2)}, u32[]{:S(2)}) collective-permute-start(bf16[2,4,136,147]{3,2,1,0:T(8,128)(2,1)} %get-tuple-element.13), channel_id=1, source_target_pairs={{1,0},{2,1},{3,2},{4,3},{5,4},{6,5},{7,6},{8,7},{9,8},{10,9},{11,1... | collective-permute-start | bytes 959624 | tf_op jit(solution)/shard_map/ppermute | solution.py:28
  28.5 1.1 %fusion.13 = (bf16[2,9,128,128]{3,2,1,0:T(8,128)(2,1)}, bf16[2,9,128,128]{3,2,1,0:T(8,128)(2,1)}) fusion(bf16[2,1,9,128,128]{4,3,2,1,0:T(8,128)(2,1)S(1)} %select_bitcast_fusion, bf16[2,1,9,128,128]{4,3,2,1,0:T(8,128)(2,1)S(1)} %bitcast.23), kind=kLoop, calls=%fused_computation.23 | loop fusion | flops 589824 | bytes 2359296 | tf_op jit(solution)/shard_map/squeeze | solution.py:149
  29.6 1.5 %collective-permute-start.2 = (bf16[2,4,136,147]{3,2,1,0:T(8,128)(2,1)S(1)}, bf16[2,4,136,147]{3,2,1,0:T(8,128)(2,1)}, u32[]{:S(2)}, u32[]{:S(2)}) collective-permute-start(bf16[2,4,136,147]{3,2,1,0:T(8,128)(2,1)S(1)} %get-tuple-element.12), channel_id=1, source_target_pairs={{0,1},{1,2},{2,3},{3,4},{4,5},{5,6},{6,7},{7,8},{8,9},{9,10},{10,1... | collective-permute-start | bytes 959624 | tf_op jit(solution)/shard_map/ppermute | solution.py:27
  31.1 20.2 %collective-permute-done.3 = bf16[2,4,136,147]{3,2,1,0:T(8,128)(2,1)S(1)} collective-permute-done((bf16[2,4,136,147]{3,2,1,0:T(8,128)(2,1)S(1)}, bf16[2,4,136,147]{3,2,1,0:T(8,128)(2,1)S(1)}, u32[]{:S(2)}, u32[]{:S(2)}) %collective-permute-start.3) | collective-permute-done | bytes 319904 | tf_op jit(solution)/shard_map/ppermute | solution.py:31
  51.4 1.0 slice.57
  52.4 0.1 slice.72
  52.6 1.0 slice.61
  53.6 0.0 copy-start.2
  53.6 1.0 slice.59
  54.6 0.2 copy.22
  54.9 0.3 copy.23
  55.2 0.0 collective-permute-done.4
  55.2 0.3 maximum_select_fusion
  55.5 0.0 collective-permute-done.2
  55.5 0.0 copy-done.2
  55.5 2.1 %fusion.1 = f32[2,16,152,147]{3,2,1,0:T(8,128)S(1)} fusion(bf16[2,4,136,147]{3,2,1,0:T(8,128)(2,1)S(1)} %maximum_select_fusion, bf16[2,4,136,147]{3,2,1,0:T(8,128)(2,1)} %collective-permute-done.2, bf16[2,8,4,147]{3,2,1,0:T(4,128)(2,1)S(1)} %collective-permute-done.1, bf16[2,8,4,147]{3,2,1,0:T(4,128)(2,1)S(1)} %copy-done.2, ...), kind=kLoop, calls=%fused_computation.4 | loop fusion | flops 17160192 | bytes 4139520 | tf_op jit(solution)/shard_map/convert_element_type | solution.py:132
  57.6 1.6 %slice.74.x_ref = f32[2,16,152,128]{3,2,1,0:T(8,128)} slice(f32[2,16,152,147]{3,2,1,0:T(8,128)S(1)} %fusion.1), slice={[0:2], [0:16], [0:152], [0:128]} | slice | bytes 4980736 | tf_op jit(solution)/shard_map/slice | solution.py:133
  59.2 1.6 %slice.75.aux_ref = f32[2,16,152,19]{3,2,1,0:T(8,128)} slice(f32[2,16,152,147]{3,2,1,0:T(8,128)S(1)} %fusion.1), slice={[0:2], [0:16], [0:152], [128:147]} | slice | bytes 739328 | tf_op jit(solution)/shard_map/slice | solution.py:134
  60.9 9.5 %shard_map.68.x_ref = f32[2,16,152,128]{3,2,1,0:T(8,128)} custom-call(f32[2,16,152,128]{3,2,1,0:T(8,128)} %slice.74.x_ref, f32[2,16,152,19]{3,2,1,0:T(8,128)} %slice.75.aux_ref, bf16[2,9,128,128]{3,2,1,0:T(8,128)(2,1)} %get-tuple-element.11.w_ref), custom_call_target="tpu_custom_call" | custom-call | flops 1123024896 | bytes 5350400 | tf_op jit(solution)/shard_map/pallas_call | solution.py:108
  70.4 8.8 %shard_map.69.x_ref = f32[2,16,152,128]{3,2,1,0:T(8,128)} custom-call(f32[2,16,152,128]{3,2,1,0:T(8,128)} %shard_map.68.x_ref, f32[2,16,152,19]{3,2,1,0:T(8,128)} %slice.75.aux_ref, bf16[2,9,128,128]{3,2,1,0:T(8,128)(2,1)} %get-tuple-element.10.w_ref), custom_call_target="tpu_custom_call" | custom-call | flops 962592768 | bytes 5350400 | tf_op jit(solution)/shard_map/pallas_call | solution.py:108
  79.1 1.4 %fusion.14 = bf16[2,8,128,128]{2,3,1,0:T(8,128)(2,1)S(1)} fusion(f32[2,16,152,128]{3,2,1,0:T(8,128)} %shard_map.69.x_ref), kind=kLoop, calls=%fused_computation.26 | loop fusion | bytes 1048576 | tf_op jit(solution)/shard_map/convert_element_type | solution.py:158
  80.5 11.2 %shard_map.70.x_ref = f32[2,16,152,128]{3,2,1,0:T(8,128)} custom-call(f32[2,16,152,128]{3,2,1,0:T(8,128)} %shard_map.69.x_ref, f32[2,16,152,19]{3,2,1,0:T(8,128)} %slice.75.aux_ref, bf16[2,9,128,128]{3,2,1,0:T(8,128)(2,1)} %get-tuple-element.10.w_ref), custom_call_target="tpu_custom_call" | custom-call | flops 802160640 | bytes 5350400 | tf_op jit(solution)/shard_map/pallas_call | solution.py:108
  91.8 1.0 copy.24
  92.8 9.9 %shard_map.71 = f32[2,16,152,128]{3,2,1,0:T(8,128)} custom-call(f32[2,16,152,128]{3,2,1,0:T(8,128)} %shard_map.70.x_ref, f32[2,16,152,19]{3,2,1,0:T(8,128)} %slice.75.aux_ref, bf16[2,9,128,128]{3,2,1,0:T(8,128)(2,1)} %get-tuple-element.11.w_ref), custom_call_target="tpu_custom_call" | custom-call | flops 641728512 | bytes 5350400 | tf_op jit(solution)/shard_map/pallas_call | solution.py:108
  102.7 1.4 %fusion.15 = bf16[2,8,128,128]{2,3,1,0:T(8,128)(2,1)S(1)} fusion(f32[2,16,152,128]{3,2,1,0:T(8,128)} %shard_map.71), kind=kLoop, calls=%fused_computation.27 | loop fusion | bytes 1048576 | tf_op jit(solution)/shard_map/convert_element_type | solution.py:175
  104.0 1.0 copy.25
  (5 shorter events, 0.2 us)
Async XLA Ops:
  0.6 9.9 %copy-start.3 = (s32[128]{0:T(128)S(1)}, s32[128]{0:T(128)}, u32[]{:S(2)}) copy-start(s32[128]{0:T(128)} %param.9) | copy-start | bytes 1540
  4.3 6.2 %collective-permute-start.1 = (bf16[2,8,4,147]{3,2,1,0:T(4,128)(2,1)S(1)}, bf16[2,8,4,147]{3,2,1,0:T(4,128)(2,1)S(1)}, u32[]{:S(2)}, u32[]{:S(2)}) collective-permute-start(bf16[2,8,4,147]{3,2,1,0:T(4,128)(2,1)S(1)} %get-tuple-element.9), channel_id=1, source_target_pairs={{16,0},{32,16},{48,32},{64,48},{80,64},{96,80},{112,96},{128,112},... | collective-permute-start | bytes 56456 | tf_op jit(solution)/shard_map/ppermute | solution.py:22
  6.7 13.1 %collective-permute-start = (bf16[2,8,4,147]{3,2,1,0:T(4,128)(2,1)S(1)}, bf16[2,8,4,147]{3,2,1,0:T(4,128)(2,1)S(1)}, u32[]{:S(2)}, u32[]{:S(2)}) collective-permute-start(bf16[2,8,4,147]{3,2,1,0:T(4,128)(2,1)S(1)} %get-tuple-element.8), channel_id=1, source_target_pairs={{0,16},{16,32},{32,48},{48,64},{64,80},{80,96},{96,112},{112,128},... | collective-permute-start | bytes 56456 | tf_op jit(solution)/shard_map/ppermute | solution.py:21
  10.5 15.5 %copy-start = (bf16[2,9,128,128]{3,2,1,0:T(8,128)(2,1)S(1)}, bf16[2,9,128,128]{3,2,1,0:T(8,128)(2,1)}, u32[]{:S(2)}) copy-start(bf16[2,9,128,128]{3,2,1,0:T(8,128)(2,1)} %param.6) | copy-start | bytes 1769476
  19.8 1.5 %copy-start.1 = (bf16[2,8,4,147]{3,2,1,0:T(4,128)(2,1)}, bf16[2,8,4,147]{3,2,1,0:T(4,128)(2,1)S(1)}, u32[]{:S(2)}) copy-start(bf16[2,8,4,147]{3,2,1,0:T(4,128)(2,1)S(1)} %collective-permute-done) | copy-start | bytes 56452
  21.4 30.0 %collective-permute-start.3 = (bf16[2,4,136,147]{3,2,1,0:T(8,128)(2,1)S(1)}, bf16[2,4,136,147]{3,2,1,0:T(8,128)(2,1)S(1)}, u32[]{:S(2)}, u32[]{:S(2)}) collective-permute-start(bf16[2,4,136,147]{3,2,1,0:T(8,128)(2,1)S(1)} %get-tuple-element.12), channel_id=1, source_target_pairs={{15,511},{31,495},{47,479},{63,463},{79,447},{95,431},{111,415},{1... | collective-permute-start | bytes 959624 | tf_op jit(solution)/shard_map/ppermute | solution.py:31
  26.4 28.8 %collective-permute-start.4 = (bf16[2,4,136,147]{3,2,1,0:T(8,128)(2,1)}, bf16[2,4,136,147]{3,2,1,0:T(8,128)(2,1)}, u32[]{:S(2)}, u32[]{:S(2)}) collective-permute-start(bf16[2,4,136,147]{3,2,1,0:T(8,128)(2,1)} %get-tuple-element.13), channel_id=1, source_target_pairs={{1,0},{2,1},{3,2},{4,3},{5,4},{6,5},{7,6},{8,7},{9,8},{10,9},{11,1... | collective-permute-start | bytes 959624 | tf_op jit(solution)/shard_map/ppermute | solution.py:28
  29.6 25.9 %collective-permute-start.2 = (bf16[2,4,136,147]{3,2,1,0:T(8,128)(2,1)S(1)}, bf16[2,4,136,147]{3,2,1,0:T(8,128)(2,1)}, u32[]{:S(2)}, u32[]{:S(2)}) collective-permute-start(bf16[2,4,136,147]{3,2,1,0:T(8,128)(2,1)S(1)} %get-tuple-element.12), channel_id=1, source_target_pairs={{0,1},{1,2},{2,3},{3,4},{4,5},{5,6},{6,7},{7,8},{8,9},{9,10},{10,1... | collective-permute-start | bytes 959624 | tf_op jit(solution)/shard_map/ppermute | solution.py:27
  53.6 1.8 %copy-start.2 = (bf16[2,8,4,147]{3,2,1,0:T(4,128)(2,1)S(1)}, bf16[2,8,4,147]{3,2,1,0:T(4,128)(2,1)}, u32[]{:S(2)}) copy-start(bf16[2,8,4,147]{3,2,1,0:T(4,128)(2,1)} %copy-done.1) | copy-start | bytes 56452

commit v2 on v1

--- a/solution.py
+++ b/solution.py
@@ -20,15 +20,24 @@
     to_left = [((i + 1) % nlon, i) for i in range(nlon)]
     from_left = lax.ppermute(block[:, :, cols - HALO :], "lon", to_right)
     from_right = lax.ppermute(block[:, :, :HALO], "lon", to_left)
+
+    top = nlat - 1
+    top_rows = block[:, rows - HALO :]
+
+    def across(piece, shift):
+        pairs = [(b * nlat + top, ((shift - b) % nlon) * nlat + top) for b in range(nlon)]
+        return lax.ppermute(piece, ("lon", "lat"), pairs)
+
+    mirror_low = across(top_rows[:, :, cols - HALO :], nlon - 2)
+    mirror_mid = across(top_rows, nlon - 1)
+    mirror_high = across(top_rows[:, :, :HALO], nlon)
+    mirrored = jnp.concatenate([mirror_low, mirror_mid, mirror_high], axis=2)
     wide = jnp.concatenate([from_left, block, from_right], axis=2)
 
     to_up = [(j, j + 1) for j in range(nlat - 1)]
     to_down = [(j + 1, j) for j in range(nlat - 1)]
     below = lax.ppermute(wide[:, rows - HALO :], "lat", to_up)
     above = lax.ppermute(wide[:, :HALO], "lat", to_down)
-    top = nlat - 1
-    mirror_pairs = [(b * nlat + top, (nlon - 1 - b) * nlat + top) for b in range(nlon)]
-    mirrored = lax.ppermute(wide[:, rows - HALO :], ("lon", "lat"), mirror_pairs)
     mirrored = mirrored[:, ::-1, ::-1]
     field_part = mirrored[..., :channels] * fold_sign
     coef_part = mirrored[..., channels : channels + layers * taps]

time: 106 us -> 109 us (1.028)
  starting transfers between devices: 14.4 us -> 28.6 us
  waiting for transfers between devices: 29.5 us -> 16.6 us
  other arithmetic: 5.28 us -> 6.44 us
    ppermute x1 -> x3, starting transfers between devices: 4.69 us -> 18.7 us  [across(): return lax.ppermute(piece, ('lon', 'lat'), pairs)]
    ppermute x1, waiting for transfers between devices: 9.27 us -> 0.01 us  [exchange(): from_left = lax.ppermute(block[:, :, cols - HALO:], 'lon', to_right)]
    ppermute x1 -> x3, waiting for transfers between devices: 20.2 us -> 16.6 us  [across(): return lax.ppermute(piece, ('lon', 'lat'), pairs)]
  transfers between devices with their start and end apart: 5 -> 7, of which waited for: 2 -> 2; matrix products, arithmetic and copies ran while one was open for 5% -> 8% of each run, Pallas kernels for 0% -> 0%
where the time goes in v2:
time: 109 us; the launch traced here: 108 us
  Pallas kernels  39.5 us (36%)
  starting transfers between devices  28.6 us (26%)
  waiting for transfers between devices  16.6 us (15%)
  local copies, waits for them, and re-layouts  16.4 us (15%)
  other arithmetic  6.44 us (6%)
    pallas_call x4, Pallas kernels, stencil(): pl.pallas_call(kernel, out_shape=jax.ShapeDtypeStruct(x.shape, jnp.float3...  39.5 us
    ppermute x3, starting transfers between devices, across(): return lax.ppermute(piece, ('lon', 'lat'), pairs)  18.7 us
    ppermute x3, waiting for transfers between devices, across(): return lax.ppermute(piece, ('lon', 'lat'), pairs)  16.6 us
    ppermute x1, starting transfers between devices, exchange(): from_left = lax.ppermute(block[:, :, cols - HALO:], 'lon', to_right)  3.94 us
    unnamed x11, local copies, waits for them, and re-layouts  3.35 us
    ppermute x1, starting transfers between devices, exchange(): from_right = lax.ppermute(block[:, :, :HALO], 'lon', to_left)  2.37 us
  transfers between devices with their start and end apart: 7, of which 2 were waited for; matrix products, arithmetic and copies ran while one was open for 8% of the time, Pallas kernels for 0%

profile of v2, /device:TPU:31, one launch (start us, length us, event | category | flops | bytes accessed | tf_op | source)
XLA Modules:
  0.0 108.4 jit_solution(18366421737040447262)
XLA Ops:
  0.6 0.7 convert_bitcast_fusion
  1.3 0.3 copy.21
  1.7 0.9 copy.19
  2.5 0.3 copy.20
  2.9 1.3 %copy.18 = bf16[2,8,128,128]{2,3,1,0:T(8,128)(2,1)S(1)} copy(bf16[2,8,128,128]{3,2,1,0:T(8,128)(2,1)} %param.5) | data formatting | bytes 1048576 | tf_op args[0]
  4.2 0.1 pad_maximum_fusion.5
  4.3 2.4 %collective-permute-start.1 = (bf16[2,8,4,147]{3,2,1,0:T(4,128)(2,1)S(1)}, bf16[2,8,4,147]{3,2,1,0:T(4,128)(2,1)S(1)}, u32[]{:S(2)}, u32[]{:S(2)}) collective-permute-start(bf16[2,8,4,147]{3,2,1,0:T(4,128)(2,1)S(1)} %get-tuple-element.11), channel_id=1, source_target_pairs={{16,0},{32,16},{48,32},{64,48},{80,64},{96,80},{112,96},{128,112},... | collective-permute-start | bytes 56456 | tf_op jit(solution)/shard_map/ppermute | solution.py:22
  6.7 0.0 copy-start.3
  6.7 0.0 copy-start
  6.7 3.9 %collective-permute-start = (bf16[2,8,4,147]{3,2,1,0:T(4,128)(2,1)S(1)}, bf16[2,8,4,147]{3,2,1,0:T(4,128)(2,1)S(1)}, u32[]{:S(2)}, u32[]{:S(2)}) collective-permute-start(bf16[2,8,4,147]{3,2,1,0:T(4,128)(2,1)S(1)} %get-tuple-element.10), channel_id=1, source_target_pairs={{0,16},{16,32},{32,48},{48,64},{64,80},{80,96},{96,112},{112,128},... | collective-permute-start | bytes 56456 | tf_op jit(solution)/shard_map/ppermute | solution.py:21
  10.6 0.1 pad_maximum_fusion.7
  10.7 12.3 %collective-permute-start.5 = (bf16[2,4,4,147]{3,2,1,0:T(4,128)(2,1)S(1)}, bf16[2,4,4,147]{3,2,1,0:T(4,128)(2,1)S(1)}, u32[]{:S(2)}, u32[]{:S(2)}) collective-permute-start(bf16[2,4,4,147]{3,2,1,0:T(4,128)(2,1)S(1)} %get-tuple-element.9), channel_id=1, source_target_pairs={{15,15},{31,511},{47,495},{63,479},{79,463},{95,447},{111,431},{12... | collective-permute-start | bytes 28232 | tf_op jit(solution)/shard_map/ppermute | solution.py:29
  23.1 0.3 pad_maximum_fusion.1
  23.4 0.8 slice.83
  24.2 1.9 %collective-permute-start.4 = (bf16[2,4,128,147]{3,2,1,0:T(8,128)(2,1)}, bf16[2,4,128,147]{3,2,1,0:T(8,128)(2,1)S(1)}, u32[]{:S(2)}, u32[]{:S(2)}) collective-permute-start(bf16[2,4,128,147]{3,2,1,0:T(8,128)(2,1)} %slice.83), channel_id=1, source_target_pairs={{15,511},{31,495},{47,479},{63,463},{79,447},{95,431},{111,415},{1... | collective-permute-start | bytes 903176 | tf_op jit(solution)/shard_map/ppermute | solution.py:29
  26.2 4.4 %collective-permute-start.3 = (bf16[2,4,4,147]{3,2,1,0:T(4,128)(2,1)S(1)}, bf16[2,4,4,147]{3,2,1,0:T(4,128)(2,1)S(1)}, u32[]{:S(2)}, u32[]{:S(2)}) collective-permute-start(bf16[2,4,4,147]{3,2,1,0:T(4,128)(2,1)S(1)} %get-tuple-element.8), channel_id=1, source_target_pairs={{15,495},{31,479},{47,463},{63,447},{79,431},{95,415},{111,399},{1... | collective-permute-start | bytes 28232 | tf_op jit(solution)/shard_map/ppermute | solution.py:29
  30.6 0.0 copy-done.3
  30.6 0.0 copy-start.2
  30.6 0.0 copy-done
  30.7 0.3 select_bitcast_fusion
  31.0 1.1 %fusion.13 = (bf16[2,9,128,128]{3,2,1,0:T(8,128)(2,1)}, bf16[2,9,128,128]{3,2,1,0:T(8,128)(2,1)}) fusion(bf16[2,1,9,128,128]{4,3,2,1,0:T(8,128)(2,1)S(1)} %select_bitcast_fusion, bf16[2,1,9,128,128]{4,3,2,1,0:T(8,128)(2,1)S(1)} %bitcast.25), kind=kLoop, calls=%fused_computation.24 | loop fusion | flops 589824 | bytes 2359296 | tf_op jit(solution)/shard_map/squeeze | solution.py:158
  32.1 0.0 collective-permute-done.1
  32.1 0.0 collective-permute-done
  32.1 0.0 copy-start.1
  32.1 0.6 pad_maximum_fusion
  32.8 0.9 fusion.17
  33.6 2.1 %collective-permute-start.6 = (bf16[2,4,136,147]{3,2,1,0:T(8,128)(2,1)}, bf16[2,4,136,147]{3,2,1,0:T(8,128)(2,1)}, u32[]{:S(2)}, u32[]{:S(2)}) collective-permute-start(bf16[2,4,136,147]{3,2,1,0:T(8,128)(2,1)} %get-tuple-element.15), channel_id=1, source_target_pairs={{1,0},{2,1},{3,2},{4,3},{5,4},{6,5},{7,6},{8,7},{9,8},{10,9},{11,1... | collective-permute-start | bytes 959624 | tf_op jit(solution)/shard_map/ppermute | solution.py:40
  35.7 1.5 %collective-permute-start.2 = (bf16[2,4,136,147]{3,2,1,0:T(8,128)(2,1)S(1)}, bf16[2,4,136,147]{3,2,1,0:T(8,128)(2,1)}, u32[]{:S(2)}, u32[]{:S(2)}) collective-permute-start(bf16[2,4,136,147]{3,2,1,0:T(8,128)(2,1)S(1)} %get-tuple-element.14), channel_id=1, source_target_pairs={{0,1},{1,2},{2,3},{3,4},{4,5},{5,6},{6,7},{7,8},{8,9},{9,10},{10,1... | collective-permute-start | bytes 959624 | tf_op jit(solution)/shard_map/ppermute | solution.py:39
  37.2 0.0 collective-permute-done.5
  37.2 12.8 %collective-permute-done.3 = bf16[2,4,4,147]{3,2,1,0:T(4,128)(2,1)S(1)} collective-permute-done((bf16[2,4,4,147]{3,2,1,0:T(4,128)(2,1)S(1)}, bf16[2,4,4,147]{3,2,1,0:T(4,128)(2,1)S(1)}, u32[]{:S(2)}, u32[]{:S(2)}) %collective-permute-start.3) | collective-permute-done | bytes 9440 | tf_op jit(solution)/shard_map/ppermute | solution.py:29
  50.0 3.8 %collective-permute-done.4 = bf16[2,4,128,147]{3,2,1,0:T(8,128)(2,1)S(1)} collective-permute-done((bf16[2,4,128,147]{3,2,1,0:T(8,128)(2,1)}, bf16[2,4,128,147]{3,2,1,0:T(8,128)(2,1)S(1)}, u32[]{:S(2)}, u32[]{:S(2)}) %collective-permute-start.4) | collective-permute-done | bytes 301088 | tf_op jit(solution)/shard_map/ppermute | solution.py:29
  53.9 0.2 pad_maximum_fusion.3
  54.1 0.0 copy-done.2
  54.1 0.0 copy-done.1
  54.1 1.0 slice.70
  55.1 0.6 broadcast_multiply_fusion
  55.7 0.1 slice.86
  55.9 1.0 slice.74
  56.9 1.0 slice.72
  57.9 0.2 copy.22
  58.2 0.3 copy.23
  58.5 0.0 collective-permute-done.6
  58.5 0.3 maximum_select_fusion
  58.7 0.0 collective-permute-done.2
  58.7 2.1 %fusion.1 = f32[2,16,152,147]{3,2,1,0:T(8,128)S(1)} fusion(bf16[2,4,136,147]{3,2,1,0:T(8,128)(2,1)S(1)} %maximum_select_fusion, bf16[2,4,136,147]{3,2,1,0:T(8,128)(2,1)} %collective-permute-done.2, bf16[2,8,4,147]{3,2,1,0:T(4,128)(2,1)S(1)} %collective-permute-done.1, bf16[2,8,4,147]{3,2,1,0:T(4,128)(2,1)} %copy-done.1, bf16[2,8,128,1]{3,2,1,0:T(8,128)(2,1)S(1)} %copy.21, ...), kind=kLoop, calls=%fused_computation.4 | loop fusion | flops 17160192 | bytes 4139520 | tf_op jit(solution)/shard_map/convert_element_type | solution.py:141
  60.9 1.7 %slice.88.x_ref = f32[2,16,152,128]{3,2,1,0:T(8,128)} slice(f32[2,16,152,147]{3,2,1,0:T(8,128)S(1)} %fusion.1), slice={[0:2], [0:16], [0:152], [0:128]} | slice | bytes 4980736 | tf_op jit(solution)/shard_map/slice | solution.py:142
  62.5 1.6 %slice.89.aux_ref = f32[2,16,152,19]{3,2,1,0:T(8,128)} slice(f32[2,16,152,147]{3,2,1,0:T(8,128)S(1)} %fusion.1), slice={[0:2], [0:16], [0:152], [128:147]} | slice | bytes 739328 | tf_op jit(solution)/shard_map/slice | solution.py:143
  64.2 9.5 %shard_map.68.x_ref = f32[2,16,152,128]{3,2,1,0:T(8,128)} custom-call(f32[2,16,152,128]{3,2,1,0:T(8,128)} %slice.88.x_ref, f32[2,16,152,19]{3,2,1,0:T(8,128)} %slice.89.aux_ref, bf16[2,9,128,128]{3,2,1,0:T(8,128)(2,1)} %get-tuple-element.13.w_ref), custom_call_target="tpu_custom_call" | custom-call | flops 1123024896 | bytes 5350400 | tf_op jit(solution)/shard_map/pallas_call | solution.py:117
  73.7 8.8 %shard_map.69.x_ref = f32[2,16,152,128]{3,2,1,0:T(8,128)} custom-call(f32[2,16,152,128]{3,2,1,0:T(8,128)} %shard_map.68.x_ref, f32[2,16,152,19]{3,2,1,0:T(8,128)} %slice.89.aux_ref, bf16[2,9,128,128]{3,2,1,0:T(8,128)(2,1)} %get-tuple-element.12.w_ref), custom_call_target="tpu_custom_call" | custom-call | flops 962592768 | bytes 5350400 | tf_op jit(solution)/shard_map/pallas_call | solution.py:117
  82.5 1.4 %fusion.14 = bf16[2,8,128,128]{2,3,1,0:T(8,128)(2,1)S(1)} fusion(f32[2,16,152,128]{3,2,1,0:T(8,128)} %shard_map.69.x_ref), kind=kLoop, calls=%fused_computation.28 | loop fusion | bytes 1048576 | tf_op jit(solution)/shard_map/convert_element_type | solution.py:167
  83.9 11.3 %shard_map.70.x_ref = f32[2,16,152,128]{3,2,1,0:T(8,128)} custom-call(f32[2,16,152,128]{3,2,1,0:T(8,128)} %shard_map.69.x_ref, f32[2,16,152,19]{3,2,1,0:T(8,128)} %slice.89.aux_ref, bf16[2,9,128,128]{3,2,1,0:T(8,128)(2,1)} %get-tuple-element.12.w_ref), custom_call_target="tpu_custom_call" | custom-call | flops 802160640 | bytes 5350400 | tf_op jit(solution)/shard_map/pallas_call | solution.py:117
  95.1 1.0 copy.24
  96.1 9.9 %shard_map.71 = f32[2,16,152,128]{3,2,1,0:T(8,128)} custom-call(f32[2,16,152,128]{3,2,1,0:T(8,128)} %shard_map.70.x_ref, f32[2,16,152,19]{3,2,1,0:T(8,128)} %slice.89.aux_ref, bf16[2,9,128,128]{3,2,1,0:T(8,128)(2,1)} %get-tuple-element.13.w_ref), custom_call_target="tpu_custom_call" | custom-call | flops 641728512 | bytes 5350400 | tf_op jit(solution)/shard_map/pallas_call | solution.py:117
  106.0 1.4 %fusion.15 = bf16[2,8,128,128]{2,3,1,0:T(8,128)(2,1)S(1)} fusion(f32[2,16,152,128]{3,2,1,0:T(8,128)} %shard_map.71), kind=kLoop, calls=%fused_computation.29 | loop fusion | bytes 1048576 | tf_op jit(solution)/shard_map/convert_element_type | solution.py:184
  107.4 1.0 copy.25
  (4 shorter events, 0.1 us)
Async XLA Ops:
  4.3 27.8 %collective-permute-start.1 = (bf16[2,8,4,147]{3,2,1,0:T(4,128)(2,1)S(1)}, bf16[2,8,4,147]{3,2,1,0:T(4,128)(2,1)S(1)}, u32[]{:S(2)}, u32[]{:S(2)}) collective-permute-start(bf16[2,8,4,147]{3,2,1,0:T(4,128)(2,1)S(1)} %get-tuple-element.11), channel_id=1, source_target_pairs={{16,0},{32,16},{48,32},{64,48},{80,64},{96,80},{112,96},{128,112},... | collective-permute-start | bytes 56456 | tf_op jit(solution)/shard_map/ppermute | solution.py:22
  6.7 23.9 %copy-start.3 = (s32[128]{0:T(128)S(1)}, s32[128]{0:T(128)}, u32[]{:S(2)}) copy-start(s32[128]{0:T(128)} %param.9) | copy-start | bytes 1540
  6.7 24.0 %copy-start = (bf16[2,9,128,128]{3,2,1,0:T(8,128)(2,1)S(1)}, bf16[2,9,128,128]{3,2,1,0:T(8,128)(2,1)}, u32[]{:S(2)}) copy-start(bf16[2,9,128,128]{3,2,1,0:T(8,128)(2,1)} %param.6) | copy-start | bytes 1769476
  6.7 25.4 %collective-permute-start = (bf16[2,8,4,147]{3,2,1,0:T(4,128)(2,1)S(1)}, bf16[2,8,4,147]{3,2,1,0:T(4,128)(2,1)S(1)}, u32[]{:S(2)}, u32[]{:S(2)}) collective-permute-start(bf16[2,8,4,147]{3,2,1,0:T(4,128)(2,1)S(1)} %get-tuple-element.10), channel_id=1, source_target_pairs={{0,16},{16,32},{32,48},{48,64},{64,80},{80,96},{96,112},{112,128},... | collective-permute-start | bytes 56456 | tf_op jit(solution)/shard_map/ppermute | solution.py:21
  10.7 26.5 %collective-permute-start.5 = (bf16[2,4,4,147]{3,2,1,0:T(4,128)(2,1)S(1)}, bf16[2,4,4,147]{3,2,1,0:T(4,128)(2,1)S(1)}, u32[]{:S(2)}, u32[]{:S(2)}) collective-permute-start(bf16[2,4,4,147]{3,2,1,0:T(4,128)(2,1)S(1)} %get-tuple-element.9), channel_id=1, source_target_pairs={{15,15},{31,511},{47,495},{63,479},{79,463},{95,447},{111,431},{12... | collective-permute-start | bytes 28232 | tf_op jit(solution)/shard_map/ppermute | solution.py:29
  24.2 29.6 %collective-permute-start.4 = (bf16[2,4,128,147]{3,2,1,0:T(8,128)(2,1)}, bf16[2,4,128,147]{3,2,1,0:T(8,128)(2,1)S(1)}, u32[]{:S(2)}, u32[]{:S(2)}) collective-permute-start(bf16[2,4,128,147]{3,2,1,0:T(8,128)(2,1)} %slice.83), channel_id=1, source_target_pairs={{15,511},{31,495},{47,479},{63,463},{79,447},{95,431},{111,415},{1... | collective-permute-start | bytes 903176 | tf_op jit(solution)/shard_map/ppermute | solution.py:29
  26.2 23.9 %collective-permute-start.3 = (bf16[2,4,4,147]{3,2,1,0:T(4,128)(2,1)S(1)}, bf16[2,4,4,147]{3,2,1,0:T(4,128)(2,1)S(1)}, u32[]{:S(2)}, u32[]{:S(2)}) collective-permute-start(bf16[2,4,4,147]{3,2,1,0:T(4,128)(2,1)S(1)} %get-tuple-element.8), channel_id=1, source_target_pairs={{15,495},{31,479},{47,463},{63,447},{79,431},{95,415},{111,399},{1... | collective-permute-start | bytes 28232 | tf_op jit(solution)/shard_map/ppermute | solution.py:29
  30.6 23.4 %copy-start.2 = (bf16[128]{0:T(256)(128)(2,1)}, bf16[128]{0:T(256)(128)(2,1)S(1)}, u32[]{:S(2)}) copy-start(bf16[128]{0:T(256)(128)(2,1)S(1)} %fusion.16) | copy-start | bytes 772
  32.1 22.0 %copy-start.1 = (bf16[2,8,4,147]{3,2,1,0:T(4,128)(2,1)}, bf16[2,8,4,147]{3,2,1,0:T(4,128)(2,1)S(1)}, u32[]{:S(2)}) copy-start(bf16[2,8,4,147]{3,2,1,0:T(4,128)(2,1)S(1)} %collective-permute-done) | copy-start | bytes 56452
  33.6 24.8 %collective-permute-start.6 = (bf16[2,4,136,147]{3,2,1,0:T(8,128)(2,1)}, bf16[2,4,136,147]{3,2,1,0:T(8,128)(2,1)}, u32[]{:S(2)}, u32[]{:S(2)}) collective-permute-start(bf16[2,4,136,147]{3,2,1,0:T(8,128)(2,1)} %get-tuple-element.15), channel_id=1, source_target_pairs={{1,0},{2,1},{3,2},{4,3},{5,4},{6,5},{7,6},{8,7},{9,8},{10,9},{11,1... | collective-permute-start | bytes 959624 | tf_op jit(solution)/shard_map/ppermute | solution.py:40
  35.7 23.0 %collective-permute-start.2 = (bf16[2,4,136,147]{3,2,1,0:T(8,128)(2,1)S(1)}, bf16[2,4,136,147]{3,2,1,0:T(8,128)(2,1)}, u32[]{:S(2)}, u32[]{:S(2)}) collective-permute-start(bf16[2,4,136,147]{3,2,1,0:T(8,128)(2,1)S(1)} %get-tuple-element.14), channel_id=1, source_target_pairs={{0,1},{1,2},{2,3},{3,4},{4,5},{5,6},{6,7},{7,8},{8,9},{9,10},{10,1... | collective-permute-start | bytes 959624 | tf_op jit(solution)/shard_map/ppermute | solution.py:39
